TPU v7x, 128 devices: a whole 4x4x4 slice. The times are simulated.
128 devices in a mesh: group: 8 (over y_lo, x), head: 16 (over y_hi, z, core).
Axes of the slice: x: 4, y: 4 (y_hi: 2, y_lo: 2; y = y_hi * 2 + y_lo), z: 4, core: 2. Of those that a mesh axis runs over, the one named last changes fastest.
Arguments:
- symbol_lookup_table: bfloat16 [65536, 2048], P(None, 'head'), may hold values from -6 to 6
- joined_linear_maps: float32 [5, 2048, 2048], P(None, 'group', 'head'), may hold values from -0.125 to 0.125
- feedforward_lookup_map: float32 [2048, 7168], P('group', 'head'), may hold values from -0.125 to 0.125
- timeblend_result_map: float32 [2048, 2048], P('head', 'group'), may hold values from -0.125 to 0.125
- feedforward_content_map: float32 [7168, 2048], P('head', 'group'), may hold values from -0.0625 to 0.0625
- lag_blend_coefs: float32 [8, 2048], replicated, may hold values from 0 to 1
- blend_narrowing_map: bfloat16 [2048, 160], replicated, may hold values from -0.125 to 0.125
- blend_widening_maps: bfloat16 [5, 32, 2048], replicated, may hold values from -0.59765625 to 0.59765625
- fading_narrowing_map: bfloat16 [2048, 64], replicated, may hold values from -0.125 to 0.125
- fading_widening_map: bfloat16 [64, 2048], P(None, 'head'), as said below
- initial_fading_power: float32 [2048], P('head'), may hold values from -12 to -2.9
- present_symbol_extra: float32 [2048], P('head'), may hold values from -3 to 3
- attender_scaling_coefs: float32 [2048], P('head'), may hold values from 0.5 to 2
- active_cluster_sheets: int32 [8], replicated, may hold values from 2 to 4, as said below
- sheets_for_inquiry: int32 [7], replicated, may hold values from 2 to 7, as said below
- sheet_symbol_indices: int32 [24, 256], replicated, may hold values from 0 to 65535
Outputs:
- hidden_states: bfloat16 [8192, 2048], P('group', 'head')
- page_states: float32 [32, 32, 4096], P('group', 'head')
- shift_edges: float32 [32, 2, 2048], P('group', None, 'head')
Inputs may be any that keep to these rules, and one draw needn't show every extreme that they name: `active_cluster_sheets`: they sum to 24; the two groups at one end of the axis, the first two or the last two, hold 4 pages each. `sheets_for_inquiry`: they sum to 24; the first page of every group but group 0 continues a request; the first or the last request holds 7 pages. `fading_widening_map`: each entry lies within 2.5 / sqrt(64) of zero.
All inputs are finite; a program needn't handle non-finite values.
Results may differ from a plain program's by a relative error of at most 0.017.
Values may be sent and summed in bfloat16 or wider, within the bound.
No kernel may reach another device: no remote copies, remote signals or barrier semaphores. Data moves between devices by JAX's collectives and lax.ppermute only.
A program may use at most 192 MiB of HBM per device.

v0:
```python
import jax
import jax.numpy as jnp
from jax import lax
from jax.sharding import PartitionSpec as P

ATTENTION_DEPTH = 64
PAGE = 256
SLOTS = 4
BLOCK = 128
EXACT_ARITHMETIC = lax.Precision.HIGHEST
LAYER_EPS = 1e-05
GROUP_EPS = 0.00064


def passed_along(value, axis, steps):
    count = lax.axis_size(axis)
    initial, last = (max(0, -steps), min(count, count - steps))
    return lax.ppermute(value, axis, [(source, source + steps) for source in range(initial, last)])


def layer_norm(value_rows):
    value_rows = value_rows.astype(jnp.float32)
    centered = value_rows - jnp.mean(value_rows, axis=-1, keepdims=True)
    return centered * lax.rsqrt(jnp.mean(centered * centered, axis=-1, keepdims=True) + LAYER_EPS)


def mixed_inputs(current, previous, lag_blend_coefs, blend_narrowing_map, blend_widening_maps):
    delta_rows = previous - current
    seeded = (current + delta_rows * lag_blend_coefs[0]).astype(jnp.bfloat16)
    low_rank = jnp.tanh(
        jnp.dot(seeded, blend_narrowing_map, preferred_element_type=jnp.float32)
    ).astype(jnp.bfloat16)
    rank_width = blend_widening_maps.shape[1]
    result_lines = []
    for number in range(5):
        column_part = low_rank[:, number * rank_width : (number + 1) * rank_width]
        offset = jnp.dot(
            column_part, blend_widening_maps[number], preferred_element_type=jnp.float32
        )
        result_lines.append(
            (current + delta_rows * (lag_blend_coefs[number + 1] + offset)).astype(jnp.bfloat16)
        )
    return result_lines


def log_decay(mixed_decay, fading_narrowing_map, fading_widening_map, initial_fading_power):
    hidden_low = jnp.tanh(
        jnp.dot(mixed_decay, fading_narrowing_map, preferred_element_type=jnp.float32)
    ).astype(jnp.bfloat16)
    return -jnp.exp(
        initial_fading_power
        + jnp.dot(hidden_low, fading_widening_map, preferred_element_type=jnp.float32)
    )


def group_norm(value_rows):
    shaped = value_rows.reshape(value_rows.shape[0], -1, ATTENTION_DEPTH)
    centered = shaped - jnp.mean(shaped, axis=-1, keepdims=True)
    normed = centered * lax.rsqrt(jnp.mean(centered * centered, axis=-1, keepdims=True) + GROUP_EPS)
    return normed.reshape(value_rows.shape)


def per_device(
    symbol_lookup_table,
    joined_linear_maps,
    feedforward_lookup_map,
    timeblend_result_map,
    feedforward_content_map,
    lag_blend_coefs,
    blend_narrowing_map,
    blend_widening_maps,
    fading_narrowing_map,
    fading_widening_map,
    initial_fading_power,
    present_symbol_extra,
    attender_scaling_coefs,
    active_cluster_sheets,
    sheets_for_inquiry,
    sheet_symbol_indices,
):
    group_count = lax.axis_size("group")
    group_here = lax.axis_index("group")
    head_here = lax.axis_index("head")
    features_on_shard = present_symbol_extra.shape[0]
    attenders_on_shard = features_on_shard // ATTENTION_DEPTH
    slot_rows = SLOTS * PAGE
    full_width = lag_blend_coefs.shape[1]
    group_number = jnp.arange(group_count, dtype=jnp.int32)
    pick_group = group_number == group_here
    live_count = jnp.sum(jnp.where(pick_group, active_cluster_sheets, 0))
    group_first = jnp.cumsum(active_cluster_sheets) - active_cluster_sheets
    first_page = jnp.sum(jnp.where(pick_group, group_first, 0))
    slot_number = jnp.arange(SLOTS, dtype=jnp.int32)
    slot_live = slot_number < live_count
    request_first = jnp.cumsum(sheets_for_inquiry) - sheets_for_inquiry
    page_here = first_page + slot_number
    begins = jnp.any(page_here[:, None] == request_first[None, :], axis=1)
    continues = jnp.where(slot_live & jnp.logical_not(begins), 1.0, 0.0).astype(jnp.float32)
    safe_page = jnp.where(slot_live, page_here, 0)
    tokens_here = jnp.take(sheet_symbol_indices, safe_page, axis=0)
    before_token = jnp.take(sheet_symbol_indices[:, -1], jnp.maximum(safe_page - 1, 0))
    own_rows = jnp.take(symbol_lookup_table, tokens_here.reshape(-1), axis=0)
    own_edges = jnp.take(symbol_lookup_table, before_token, axis=0)
    embedded, edge_rows = (
        lax.all_gather(own_rows, "head", axis=1, tiled=True),
        lax.all_gather(own_edges, "head", axis=1, tiled=True),
    )
    stack_half = joined_linear_maps.astype(jnp.bfloat16)
    key_half = feedforward_lookup_map.astype(jnp.bfloat16)
    output_half = timeblend_result_map.astype(jnp.bfloat16)
    value_half = feedforward_content_map.astype(jnp.bfloat16)
    projections, key_weight, output_weight, value_weight = (
        lax.all_gather(stack_half, "group", axis=1, tiled=True),
        lax.all_gather(key_half, "group", axis=0, tiled=True),
        lax.all_gather(output_half, "group", axis=1, tiled=True),
        lax.all_gather(value_half, "group", axis=1, tiled=True),
    )
    current = layer_norm(embedded)
    edge_first = layer_norm(edge_rows) * continues[:, None]
    current_pages = current.reshape(SLOTS, PAGE, full_width)
    previous = jnp.concatenate([edge_first[:, None, :], current_pages[:, :-1, :]], axis=1).reshape(
        slot_rows, full_width
    )
    mixed_decay, mixed_key, mixed_value, mixed_query, mixed_gate = mixed_inputs(
        current, previous, lag_blend_coefs, blend_narrowing_map, blend_widening_maps
    )
    fading_multipliers = log_decay(
        mixed_decay, fading_narrowing_map, fading_widening_map, initial_fading_power
    )
    acceptance_lines = jnp.dot(mixed_query, projections[0], preferred_element_type=jnp.float32)
    present_lookups = jnp.dot(mixed_key, projections[1], preferred_element_type=jnp.float32)
    present_contents = jnp.dot(mixed_value, projections[2], preferred_element_type=jnp.float32)
    gate_raw = jnp.dot(mixed_gate, projections[3], preferred_element_type=jnp.float32)
    gating = jax.nn.silu(gate_raw)
    blocks = slot_rows // BLOCK
    per_page = PAGE // BLOCK

    def to_blocks(value_rows):
        return value_rows.reshape(blocks, BLOCK, attenders_on_shard, ATTENTION_DEPTH).transpose(
            0, 2, 1, 3
        )

    block_index = jnp.arange(blocks, dtype=jnp.int32)
    block_start = block_index % per_page == 0
    block_slot = block_index // per_page
    slot_keep = continues * (slot_number > 0)
    keep_state = jnp.where(block_start, jnp.take(slot_keep, block_slot), 1.0)
    keep_factor = jnp.where(block_start, jnp.take(continues, block_slot), 1.0)
    attender_extra = present_symbol_extra.reshape(attenders_on_shard, ATTENTION_DEPTH)
    strictly_lower = jnp.arange(BLOCK)[:, None] > jnp.arange(BLOCK)[None, :]

    def decay_block(retained_memory, inputs):
        sequential_sweep, factor = retained_memory
        segment_askers, segment_lookups, value_block, decay_rows, keep_one, keep_two = inputs
        sequential_sweep = sequential_sweep * keep_one
        factor = factor * keep_two
        inclusive = jnp.cumsum(decay_rows, axis=1)
        exclusive = inclusive - decay_rows
        query_scaled = segment_askers * jnp.exp(exclusive)
        key_scaled = segment_lookups * jnp.exp(-inclusive)
        scores = jnp.einsum("hts,hus->htu", query_scaled, key_scaled, precision=EXACT_ARITHMETIC)
        scores = jnp.where(strictly_lower, scores, 0.0)
        selfpair_contribution = jnp.sum(
            segment_askers * attender_extra[:, None, :] * segment_lookups, axis=2
        )
        sublevel_result = (
            jnp.einsum("htu,huj->htj", scores, value_block, precision=EXACT_ARITHMETIC)
            + selfpair_contribution[:, :, None] * value_block
            + jnp.einsum("hts,hsj->htj", query_scaled, sequential_sweep, precision=EXACT_ARITHMETIC)
        )
        block_total = inclusive[:, -1, :]
        key_end = segment_lookups * jnp.exp(block_total[:, None, :] - inclusive)
        sequential_sweep = jnp.exp(block_total)[:, :, None] * sequential_sweep + jnp.einsum(
            "hts,htj->hsj", key_end, value_block, precision=EXACT_ARITHMETIC
        )
        carry_rows = query_scaled * factor[:, None, :]
        factor = factor * jnp.exp(block_total)
        return ((sequential_sweep, factor), (sublevel_result, carry_rows, sequential_sweep, factor))

    start_state = jnp.zeros((attenders_on_shard, ATTENTION_DEPTH, ATTENTION_DEPTH), jnp.float32)
    start_factor = jnp.ones((attenders_on_shard, ATTENTION_DEPTH), jnp.float32)
    final_carry, (block_out, carry_rows, block_states, block_factors) = lax.scan(
        decay_block,
        (start_state, start_factor),
        (
            to_blocks(acceptance_lines),
            to_blocks(present_lookups),
            to_blocks(present_contents),
            to_blocks(fading_multipliers),
            keep_state,
            keep_factor,
        ),
    )
    page_end = block_states[per_page - 1 :: per_page]
    page_factor = block_factors[per_page - 1 :: per_page]
    last_pick = (slot_number == live_count - 1).astype(jnp.float32)
    leaving_state = jnp.einsum("s,shij->hij", last_pick, page_end, precision=EXACT_ARITHMETIC)
    leaving_factor = jnp.einsum("s,shi->hi", last_pick, page_factor, precision=EXACT_ARITHMETIC)

    def relay_step(turn_number, incoming):
        return passed_along(
            (leaving_factor[:, :, None] * incoming + leaving_state).astype(jnp.bfloat16), "group", 1
        ).astype(jnp.float32)

    incoming = lax.fori_loop(0, group_count - 1, relay_step, jnp.zeros_like(leaving_state))
    block_out = block_out + jnp.einsum(
        "bhts,hsj->bhtj", carry_rows, incoming, precision=EXACT_ARITHMETIC
    )
    page_end = page_end + page_factor[:, :, :, None] * incoming[None]
    attended = block_out.transpose(0, 2, 1, 3).reshape(slot_rows, features_on_shard)
    normed = (group_norm(attended) * attender_scaling_coefs * gating).astype(jnp.bfloat16)
    mixer_total = lax.psum(
        jnp.dot(normed, output_weight, preferred_element_type=jnp.float32).astype(jnp.bfloat16),
        "head",
    ).astype(jnp.float32)
    residual = (embedded.astype(jnp.float32) + mixer_total).astype(jnp.bfloat16)
    last_residual = lax.dynamic_slice_in_dim(residual, live_count * PAGE - 1, 1, 0)
    arriving = passed_along(last_residual, "group", 1)
    channel_in = layer_norm(residual)
    channel_pages = channel_in.reshape(SLOTS, PAGE, full_width)
    edge_two = (
        jnp.concatenate([layer_norm(arriving), channel_pages[:-1, -1, :]], axis=0)
        * continues[:, None]
    )
    channel_prev = jnp.concatenate(
        [edge_two[:, None, :], channel_pages[:, :-1, :]], axis=1
    ).reshape(slot_rows, full_width)
    channel_delta = channel_prev - channel_in
    key_input = (channel_in + channel_delta * lag_blend_coefs[6]).astype(jnp.bfloat16)
    gate_input = (channel_in + channel_delta * lag_blend_coefs[7]).astype(jnp.bfloat16)
    gate_raw_two = jnp.dot(gate_input, projections[4], preferred_element_type=jnp.float32)
    key_raw = jnp.dot(key_input, key_weight, preferred_element_type=jnp.float32)
    squared = jnp.square(jax.nn.relu(key_raw)).astype(jnp.bfloat16)
    channel = lax.psum_scatter(
        jnp.dot(squared, value_weight, preferred_element_type=jnp.float32).astype(jnp.bfloat16),
        "head",
        scatter_dimension=1,
        tiled=True,
    ).astype(jnp.float32)
    gate_two = jax.nn.sigmoid(gate_raw_two)
    residual_local = lax.dynamic_slice_in_dim(
        residual, head_here * features_on_shard, features_on_shard, 1
    )
    hidden = (residual_local.astype(jnp.float32) + gate_two * channel).astype(jnp.bfloat16)
    row_live = jnp.repeat(slot_live, PAGE)
    hidden_out = jnp.where(row_live[:, None], hidden, jnp.zeros_like(hidden))
    state_out = page_end.reshape(SLOTS, attenders_on_shard, ATTENTION_DEPTH * ATTENTION_DEPTH)
    state_out = jnp.where(slot_live[:, None, None], state_out, jnp.zeros_like(state_out))
    first_edge = lax.dynamic_slice_in_dim(
        current_pages[:, -1, :], head_here * features_on_shard, features_on_shard, 1
    )
    second_edge = lax.dynamic_slice_in_dim(
        channel_pages[:, -1, :], head_here * features_on_shard, features_on_shard, 1
    )
    edge_out = jnp.stack([first_edge, second_edge], axis=1)
    edge_out = jnp.where(slot_live[:, None, None], edge_out, jnp.zeros_like(edge_out))
    return (hidden_out, state_out, edge_out)


def solution(mesh):
    in_specs = (
        P(None, "head"),
        P(None, "group", "head"),
        P("group", "head"),
        P("head", "group"),
        P("head", "group"),
        P(),
        P(),
        P(),
        P(),
        P(None, "head"),
        P("head"),
        P("head"),
        P("head"),
        P(),
        P(),
        P(),
    )
    out_specs = (P("group", "head"), P("group", "head", None), P("group", None, "head"))
    return jax.shard_map(
        per_device, mesh=mesh, in_specs=in_specs, out_specs=out_specs, check_vma=False
    )
```

profile of v0, /device:TPU:0, one launch (start us, length us, event | category | flops | bytes accessed | tf_op | source)
XLA Modules:
  0.0 668.3 jit_solution(10876387743382121126)
XLA Ops:
  7.2 1.9 convert_element_type.97
  15.4 10.8 %gather_fusion.1 = bf16[1024,128]{1,0:T(8,128)(2,1)S(1)} fusion(bf16[65536,128]{1,0:T(8,128)(2,1)} %param.22, s32[1024]{0:T(1024)S(1)} %broadcast_clamp_fusion), kind=kCustom, calls=%fused_computation.3 | custom fusion | bytes 528384 | tf_op jit(solution)/shard_map/jit(_take)/gather | solution.py:102
  36.4 8.6 %gather_fusion.3 = bf16[4,128]{1,0:T(4,128)(2,1)S(1)} fusion(bf16[65536,128]{1,0:T(8,128)(2,1)} %param.22, s32[1024]{0:T(1024)S(1)} %pad_clamp_fusion.1), kind=kCustom, calls=%fused_computation.5 | custom fusion | bytes 2064 | tf_op jit(solution)/shard_map/jit(_take)/gather | solution.py:103
  46.5 25.8 %all_gather.19 = bf16[4,2048]{1,0:T(4,128)(2,1)S(1)} all-gather(bf16[4,128]{1,0:T(4,128)(2,1)S(1)} %broadcast_select_fusion.2), channel_id=1, replica_groups=mesh['group'=8,'head'=16] {'head'}, dimensions={1}, use_global_device_ids=true | all-gather | bytes 17408 | tf_op jit(solution)/shard_map/all_gather | solution.py:106
  73.7 29.2 %all_gather.21 = bf16[128,2048]{1,0:T(8,128)(2,1)S(1)} all-gather(bf16[128,256]{1,0:T(8,128)(2,1)S(1)} %convert_element_type.102), channel_id=1, replica_groups=mesh['group'=8,'head'=16] {'group'}, dimensions={1}, use_global_device_ids=true | all-gather | bytes 589824 | tf_op jit(solution)/shard_map/all_gather | solution.py:115
  104.2 2.3 slice_bitcast_fusion.4
  108.2 6.0 all-gather.5.cloned.1.call-done
  114.1 3.0 convert_reduce_fusion
  117.1 3.4 fusion.32
  121.5 4.7 pad_maximum_fusion
  127.2 4.7 bitcast_subtract_fusion.2
  131.9 2.7 fusion.49
  135.1 8.0 %fusion.56 = bf16[1024,64]{0,1:T(8,128)(2,1)S(1)} fusion(bf16[2048,64]{0,1:T(8,128)(2,1)} %param.30, f32[1024,2048]{1,0:T(8,128)} %copy-done.4, bf16[1024,2048]{1,0:T(8,128)(2,1)} %all-gather.5.cloned.1.call-done, f32[2048]{0:T(1024)S(1)} %bitcast.323, f32[1024]{0:T(1024)S(1)} %add_rsqrt_fusion.1, f32[1024]{0:T(1024)S(1)} %broadcast_multiply_fusion.2, ...), kind=kOutput, calls=%fused_computation.107 | convolution fusion | flops 417398784 | bytes 13189120 | tf_op jit(solution)/shard_map/dot_general | solution.py:48
  144.4 1.9 copy.138
  146.4 6.0 add_convert_fusion.3
  152.4 2.4 convolution_bitcast_fusion.1
  154.8 3.6 add_convert_fusion.4
  159.9 3.6 add_convert_fusion.5
  165.0 74.7 %while.32 = (s32[]{:T(128)}, f32[2,64,64]{2,1,0:T(8,128)S(1)}, f32[2,64]{1,0:T(2,128)S(1)}, f32[8,2,128,64]{2,3,0,1:T(8,128)}, f32[8,2,128,64]{3,2,0,1:T(8,128)}...) while((s32[]{:T(128)}, f32[2,64,64]{2,1,0:T(8,128)S(1)}, ...), condition=%wide.region_12.14_spmd.clone, body=%wide.region_9.13_spmd.clone.sunk | while | flops 77955200 | bytes 2999012 | solution.py:182
  170.5 1.7 fusion.134
  172.2 1.7 bitcast_dynamic-update-slice_fusion.4
  179.8 1.7 fusion.134
  181.5 1.7 bitcast_dynamic-update-slice_fusion.4
  189.1 1.7 fusion.134
  190.8 1.7 bitcast_dynamic-update-slice_fusion.4
  198.5 1.7 fusion.134
  200.1 1.7 bitcast_dynamic-update-slice_fusion.4
  207.8 1.7 fusion.134
  209.4 1.7 bitcast_dynamic-update-slice_fusion.4
  217.1 1.7 fusion.134
  218.7 1.7 bitcast_dynamic-update-slice_fusion.4
  226.4 1.7 fusion.134
  228.1 1.7 bitcast_dynamic-update-slice_fusion.4
  235.7 1.7 fusion.134
  237.4 1.7 bitcast_dynamic-update-slice_fusion.4
  241.4 43.2 %while.33 = (s32[]{:T(128)}, f32[2,64,64]{2,1,0:T(8,128)S(1)}, f32[2,64]{1,0:T(2,128)S(1)}, f32[2,64,64]{2,1,0:T(8,128)S(1)}, s32[]{:T(128)}, /*index=5*/s32[]{:T(128)}) while((s32[]{:T(128)}, f32[2,64,64]{2,1,0:T(8,128)S(1)}, f32[2,64]{1,0:T(2,128)S(1)}, f32[2,64,64]{2,1,0:T(8,128)S(1)}, s32[]{:T(128)}, ...), condition=%wide.region_14.16_spmd.clone, body=%wide.region_13.15_spmd.clone.sunk | while | flops 40963 | bytes 197239 | solution.py:205
  241.5 2.2 collective-permute-start
  243.7 1.6 collective-permute-done
  245.4 4.2 collective-permute-start
  249.6 1.6 collective-permute-done
  251.3 4.2 collective-permute-start
  255.6 1.6 collective-permute-done
  257.2 4.2 collective-permute-start
  261.5 1.6 collective-permute-done
  263.1 4.2 collective-permute-start
  267.4 1.6 collective-permute-done
  269.0 6.0 collective-permute-start
  275.0 1.6 collective-permute-done
  276.7 6.3 collective-permute-start
  284.6 2.7 fusion.109
  289.9 7.7 %multiply_convert_fusion.1 = bf16[1024,128]{1,0:T(8,128)(2,1)S(1)} fusion(bf16[5,2048,128]{2,1,0:T(8,128)(2,1)} %all-gather.7.cloned.1.call-done, f32[1024,2048]{1,0:T(8,128)} %copy-done.4, bf16[1024,2048]{1,0:T(8,128)(2,1)} %all-gather.5.cloned.1.call-done, f32[2048]{0:T(1024)S(1)} %bitcast.322, f32[1024]{0:T(1024)S(1)} %add_rsqrt_fusion.1, ...), kind=kOutput, calls=%fused_computation.114 | convolution fusion | flops 686948352 | bytes 15155712 | tf_op jit(solution)/shard_map/dot_general | solution.py:133
  297.6 3.2 convolution_convert_fusion.1
  303.1 156.8 %all-reduce.2.cloned.1.call-done = bf16[1024,2048]{1,0:T(8,128)(2,1)} async-done(((bf16[1024,2048]{1,0:T(8,128)(2,1)}), bf16[1024,2048]{1,0:T(8,128)(2,1)}) %all-reduce.2.cloned.1.call-update) | async-done | bytes 4194320 | tf_op jit(solution)/shard_map/psum | solution.py:212
  459.9 4.8 convert_reduce_fusion.1
  466.0 3.6 collective-permute-start.1
  470.5 3.2 copy-done.7
  476.4 4.7 pad_maximum_fusion.1
  481.1 4.5 bitcast_subtract_fusion.1
  485.6 18.9 %all-gather.9.cloned.1.call-done = bf16[2048,448]{0,1:T(8,128)(2,1)} async-done(((bf16[256,448]{0,1:T(8,128)(2,1)}), bf16[2048,448]{0,1:T(8,128)(2,1)}) %all-gather.9.cloned.1.call-update) | async-done | bytes 1835024 | tf_op jit(solution)/shard_map/all_gather | solution.py:114
  504.6 46.5 %all-gather.11.cloned.1.call-done = bf16[448,2048]{1,0:T(8,128)(2,1)} async-done(((bf16[448,256]{1,0:T(8,128)(2,1)}), bf16[448,2048]{1,0:T(8,128)(2,1)}) %all-gather.11.cloned.1.call-update) | async-done | bytes 1835024 | tf_op jit(solution)/shard_map/all_gather | solution.py:116
  551.1 12.2 %convolution_convert_fusion = bf16[1024,2048]{1,0:T(8,128)(2,1)} fusion(bf16[448,2048]{1,0:T(8,128)(2,1)} %all-gather.11.cloned.1.call-done, bf16[2048,448]{0,1:T(8,128)(2,1)} %all-gather.9.cloned.1.call-done, f32[1024,2048]{1,0:T(8,128)} %bitcast_subtract_fusion.1, f32[2048]{0:T(1024)S(1)} %bitcast.321, bf16[1024,2048]{1,0:T(8,128)(2,1)} %copy-done.5, ...), kind=kOutput, calls=%fused_computation.83 | convolution fusion | flops 3774152704 | bytes 20463616 | tf_op jit(solution)/shard_map/dot_general | solution.py:235
  563.3 6.5 copy.116
  574.3 78.4 %reduce-scatter.4.cloned.1.call-done = bf16[128,1024]{1,0:T(8,128)(2,1)} async-done(((bf16[2048,1024]{1,0:T(8,128)(2,1)}), bf16[128,1024]{1,0:T(8,128)(2,1)}) %reduce-scatter.4.cloned.1.call-update) | async-done | bytes 262160
  653.9 7.3 %fusion.57 = bf16[1024,128]{1,0:T(8,128)(2,1)} fusion(f32[1024,2048]{1,0:T(8,128)} %bitcast_subtract_fusion.1, f32[2048]{0:T(1024)S(1)} %bitcast.320, bf16[5,2048,128]{2,1,0:T(8,128)(2,1)} %all-gather.7.cloned.1.call-done, bf16[1024,128]{1,0:T(8,128)(2,1)S(1)} %copy.117, bf16[1024,2048]{1,0:T(8,128)(2,1)} %copy-done.5, s32[]{:T(128)S(6)} %select_n.209, ...), kind=kOutput, calls=%fused_computation.108 | convolution fusion | flops 550633472 | bytes 13911044 | tf_op jit(solution)/shard_map/dot_general | solution.py:231
  (298 shorter events, 93.0 us)
Async XLA Ops:
  7.2 124.7 %copy-start = (bf16[2048,160]{0,1:T(8,128)(2,1)S(1)}, bf16[2048,160]{0,1:T(8,128)(2,1)}, u32[]{:S(2)}) copy-start(bf16[2048,160]{0,1:T(8,128)(2,1)} %param.28) | copy-start | bytes 1966084
  7.2 97.0 %all-gather.7.cloned.1.call-start = ((), (), s32[]{:S(2)}) async-start(), calls=%async_computation.2 | async-start | bytes 2949120 | tf_op jit(solution)/shard_map/all_gather | solution.py:113
  9.2 105.0 %all-gather.5.cloned.1.call-start = ((), (), s32[]{:S(2)}) async-start(), calls=%async_computation.1 | async-start | bytes 4456448 | tf_op jit(solution)/shard_map/all_gather | solution.py:105
  27.2 432.7 %all-reduce.2.cloned.1.call-start = ((), (), s32[]{:S(2)}) async-start(), calls=%async_computation.3 | async-start | bytes 8388608 | tf_op jit(solution)/shard_map/psum | solution.py:212
  114.1 6.4 copy-start.2
  121.5 5.7 copy-start.8
  131.8 3.2 copy-start.4
  135.1 24.8 %copy-start.12 = (bf16[1024,160]{0,1:T(8,128)(2,1)}, bf16[1024,160]{0,1:T(8,128)(2,1)S(1)}, u32[]{:S(2)}) copy-start(bf16[1024,160]{0,1:T(8,128)(2,1)S(1)} %fusion.49) | copy-start | bytes 983044
  135.1 8.0 %copy-start.13 = (bf16[64,128]{1,0:T(8,128)(2,1)S(1)}, bf16[64,128]{1,0:T(8,128)(2,1)}, u32[]{:S(2)}) copy-start(bf16[64,128]{1,0:T(8,128)(2,1)} %param.31) | copy-start | bytes 49156
  135.1 8.0 %copy-start.14 = (f32[128]{0:T(128)S(1)}, f32[128]{0:T(128)}, u32[]{:S(2)}) copy-start(f32[128]{0:T(128)} %param.32) | copy-start | bytes 1540
  146.4 8.4 %slice-start = ((s8[8388608]{0:T(1024)(128)(4,1)}), s8[4194304]{0:T(1024)(128)(4,1)S(1)}, s32[]{:S(2)}) async-start(s8[8388608]{0:T(1024)(128)(4,1)} %bitcast.287), calls=%async_computation.7 | async-start | bytes 8388608
  146.4 8.4 %copy-start.3 = (bf16[1024,2048]{1,0:T(8,128)(2,1)S(1)}, bf16[1024,2048]{1,0:T(8,128)(2,1)}, u32[]{:S(2)}) copy-start(bf16[1024,2048]{1,0:T(8,128)(2,1)} %all-gather.5.cloned.1.call-done) | copy-start | bytes 12582916
  146.4 8.4 %slice-start.1 = ((s8[8388608]{0:T(1024)(128)(4,1)}), s8[4194304]{0:T(1024)(128)(4,1)S(1)}, s32[]{:S(2)}) async-start(s8[8388608]{0:T(1024)(128)(4,1)} %bitcast.287), calls=%async_computation.8 | async-start | bytes 8388608
  159.9 5.1 copy-start.15
  239.8 50.1 %copy-start.16 = (f32[128]{0:T(128)S(1)}, f32[128]{0:T(128)}, u32[]{:S(2)}) copy-start(f32[128]{0:T(128)} %param.34) | copy-start | bytes 1540
  241.5 3.8 collective-permute-start
  245.4 5.8 collective-permute-start
  251.3 5.8 collective-permute-start
  257.2 5.8 collective-permute-start
  263.1 5.8 collective-permute-start
  269.0 7.6 %collective-permute-start = (bf16[2,64,64]{2,1,0:T(8,128)(2,1)S(1)}, bf16[2,64,64]{2,1,0:T(8,128)(2,1)S(1)}, u32[]{:S(2)}, u32[]{:S(2)}) collective-permute-start(bf16[2,64,64]{2,1,0:T(8,128)(2,1)S(1)} %fusion.135), channel_id=1, source_target_pairs={{0,16},{16,32},{32,48},{48,64},{64,80},{80,96},{96,112},{1,17},{17... | collective-permute-start | bytes 49160 | tf_op jit(solution)/shard_map/while/body/eval_jaxpr/ppermute | solution.py:18
  276.7 7.9 %collective-permute-start = (bf16[2,64,64]{2,1,0:T(8,128)(2,1)S(1)}, bf16[2,64,64]{2,1,0:T(8,128)(2,1)S(1)}, u32[]{:S(2)}, u32[]{:S(2)}) collective-permute-start(bf16[2,64,64]{2,1,0:T(8,128)(2,1)S(1)} %fusion.135), channel_id=1, source_target_pairs={{0,16},{16,32},{32,48},{48,64},{64,80},{80,96},{96,112},{1,17},{17... | collective-permute-start | bytes 49160 | tf_op jit(solution)/shard_map/while/body/eval_jaxpr/ppermute | solution.py:18
  297.6 3.3 copy-start.10
  297.6 4.1 copy-start.11
  300.8 203.8 %all-gather.9.cloned.1.call-start = ((), (), s32[]{:S(2)}) async-start(), calls=%async_computation.4 | async-start | bytes 2064384 | tf_op jit(solution)/shard_map/all_gather | solution.py:114
  301.6 249.5 %all-gather.11.cloned.1.call-start = ((), (), s32[]{:S(2)}) async-start(), calls=%async_computation.5 | async-start | bytes 2064384 | tf_op jit(solution)/shard_map/all_gather | solution.py:116
  302.4 350.3 %reduce-scatter.4.cloned.1.call-start = ((), (), s32[]{:S(2)}) async-start(), calls=%async_computation.6 | async-start | bytes 4456448
  464.7 5.8 copy-start.5
  466.0 7.8 %collective-permute-start.1 = (bf16[1,2048]{1,0:T(2,128)(2,1)S(1)}, bf16[1,2048]{1,0:T(2,128)(2,1)S(1)}, u32[]{:S(2)}, u32[]{:S(2)}) collective-permute-start(bf16[1,2048]{1,0:T(2,128)(2,1)S(1)} %constant_dynamic-slice_fusion.5), channel_id=1, source_target_pairs={{0,16},{16,32},{32,48},{48,64},{64,80},{80,96},{96,112},{1,17},{17... | collective-permute-start | bytes 12296 | tf_op jit(solution)/shard_map/ppermute | solution.py:18
  470.5 3.2 copy-start.7
  476.4 4.7 copy-start.6
  563.3 8.2 %copy-start.9 = (f32[8,2,64,64]{3,2,1,0:T(8,128)S(1)}, f32[8,2,64,64]{3,2,1,0:T(8,128)}, u32[]{:S(2)}) copy-start(f32[8,2,64,64]{3,2,1,0:T(8,128)} %get-tuple-element.108) | copy-start | bytes 786436
  652.7 8.5 %copy-start.1 = (bf16[2048,160]{0,1:T(8,128)(2,1)S(1)}, bf16[2048,160]{0,1:T(8,128)(2,1)}, u32[]{:S(2)}) copy-start(bf16[2048,160]{0,1:T(8,128)(2,1)} %param.28) | copy-start | bytes 1966084
Sparse Core Ops, SparseCore 0:
  9.6 43.9 all-gather.6
  56.5 57.5 all-gather.4
  300.9 158.9 all-reduce.1
  461.3 43.1 all-gather.8
  506.6 44.4 all-gather.10
  569.9 82.7 reduce-scatter.3
where the time goes:
time: 678 us; the launch traced here: 668 us
  waiting for transfers between devices  318 us (47%)
  matrix products  96 us (14%)
  local copies, waits for them, and re-layouts  78.1 us (12%)
  other arithmetic  67.8 us (10%)
  blocking collectives  55 us (8%)
  starting transfers between devices  35.3 us (5%)
  between operations  17.7 us (3%)
    psum x1, waiting for transfers between devices, per_device(): lax.psum(jnp.dot(normed, output_weight, preferred_element_type=jnp.float3...  157 us
    unnamed x7, waiting for transfers between devices  78.5 us
    all_gather x1, waiting for transfers between devices, per_device(): lax.all_gather(value_half, 'group', axis=1, tiled=True)  46.5 us
    ppermute x8, starting transfers between devices, passed_along(): lax.ppermute(value, axis, [(source, source + steps) for source in range(i...  35 us
    all_gather x1, blocking collectives, per_device(): lax.all_gather(output_half, 'group', axis=1, tiled=True)  29.2 us
    dynamic_slice x56, local copies, waits for them, and re-layouts, per_device(): lax.scan(decay_block, (start_state, start_factor), (to_blocks(acceptance_...  27.3 us
    all_gather x1, blocking collectives, per_device(): lax.all_gather(own_edges, 'head', axis=1, tiled=True)  25.8 us
    all_gather x1, waiting for transfers between devices, per_device(): lax.all_gather(key_half, 'group', axis=0, tiled=True)  18.9 us
  transfers between devices with their start and end apart: 14, of which 12 were waited for; matrix products, arithmetic and copies ran while one was open for 10% of the time, Pallas kernels for 0%

commit v1 on v0

--- a/solution.py
+++ b/solution.py
@@ -10,6 +10,13 @@
 EXACT_ARITHMETIC = lax.Precision.HIGHEST
 LAYER_EPS = 1e-05
 GROUP_EPS = 0.00064
+
+
+def chunk_pass(original):
+    u_next = tuple((original for _ in range(lax.axis_size("group"))))
+    next_value = jnp.stack(u_next)
+    carry_out = lax.all_to_all(next_value, "group", 0, 0)
+    return jnp.concatenate(carry_out, 1)
 
 
 def passed_along(value, axis, steps):
@@ -113,7 +120,7 @@
         lax.all_gather(stack_half, "group", axis=1, tiled=True),
         lax.all_gather(key_half, "group", axis=0, tiled=True),
         lax.all_gather(output_half, "group", axis=1, tiled=True),
-        lax.all_gather(value_half, "group", axis=1, tiled=True),
+        chunk_pass(value_half),
     )
     current = layer_norm(embedded)
     edge_first = layer_norm(edge_rows) * continues[:, None]

time: 678 us -> 629 us (0.928)
  waiting for transfers between devices: 318 us -> 264 us
  starting transfers between devices: 35.3 us -> 49.8 us
    all_gather x1 -> x0, waiting for transfers between devices: 46.5 us -> none  [per_device(): lax.all_gather(value_half, 'group', axis=1, tiled=True)]
    psum x1, waiting for transfers between devices: 157 us -> 134 us  [per_device(): lax.psum(jnp.dot(normed, output_weight, preferred_element_type=jnp.float3...]
    all_to_all x0 -> x1, waiting for transfers between devices: none -> 16 us  [chunk_pass(): carry_out = lax.all_to_all(next_value, 'group', 0, 0)]
    all_to_all x0 -> x1, starting transfers between devices: none -> 14.9 us  [chunk_pass(): carry_out = lax.all_to_all(next_value, 'group', 0, 0)]
    unnamed x45 -> x57, local copies, waits for them, and re-layouts: 14.5 us -> 15.4 us
    unnamed x7 -> x6, waiting for transfers between devices: 78.5 us -> 78.5 us
  transfers between devices with their start and end apart: 14 -> 14, of which waited for: 12 -> 12; matrix products, arithmetic and copies ran while one was open for 10% -> 11% of each run, Pallas kernels for 0% -> 0%
where the time goes in v1:
time: 629 us; the launch traced here: 620 us
  waiting for transfers between devices  264 us (42%)
  matrix products  94.5 us (15%)
  local copies, waits for them, and re-layouts  75.8 us (12%)
  other arithmetic  62.1 us (10%)
  blocking collectives  55 us (9%)
  starting transfers between devices  49.8 us (8%)
  between operations  17.5 us (3%)
    psum x1, waiting for transfers between devices, per_device(): lax.psum(jnp.dot(normed, output_weight, preferred_element_type=jnp.float3...  134 us
    unnamed x6, waiting for transfers between devices  78.5 us
    ppermute x8, starting transfers between devices, passed_along(): lax.ppermute(value, axis, [(source, source + steps) for source in range(i...  34.8 us
    all_gather x1, blocking collectives, per_device(): lax.all_gather(output_half, 'group', axis=1, tiled=True)  29.2 us
    all_gather x1, blocking collectives, per_device(): lax.all_gather(own_edges, 'head', axis=1, tiled=True)  25.8 us
    dynamic_slice x56, local copies, waits for them, and re-layouts, per_device(): lax.scan(decay_block, (start_state, start_factor), (to_blocks(acceptance_...  20.5 us
    all_gather x1, waiting for transfers between devices, per_device(): lax.all_gather(key_half, 'group', axis=0, tiled=True)  19.4 us
    all_to_all x1, waiting for transfers between devices, chunk_pass(): carry_out = lax.all_to_all(next_value, 'group', 0, 0)  16 us
  transfers between devices with their start and end apart: 14, of which 12 were waited for; matrix products, arithmetic and copies ran while one was open for 11% of the time, Pallas kernels for 0%

profile of v1, /device:TPU:0, one launch (start us, length us, event | category | flops | bytes accessed | tf_op | source)
XLA Modules:
  0.0 619.6 jit_solution(9119589961716809031)
XLA Ops:
  7.2 1.9 convert_element_type.97
  15.4 10.9 %gather_fusion.1 = bf16[1024,128]{1,0:T(8,128)(2,1)S(1)} fusion(bf16[65536,128]{1,0:T(8,128)(2,1)} %param.22, s32[1024]{0:T(1024)S(1)} %broadcast_clamp_fusion), kind=kCustom, calls=%fused_computation.3 | custom fusion | bytes 528384 | tf_op jit(solution)/shard_map/jit(_take)/gather | solution.py:109
  36.5 8.6 %gather_fusion.3 = bf16[4,128]{1,0:T(4,128)(2,1)S(1)} fusion(bf16[65536,128]{1,0:T(8,128)(2,1)} %param.22, s32[1024]{0:T(1024)S(1)} %pad_clamp_fusion.1), kind=kCustom, calls=%fused_computation.5 | custom fusion | bytes 2064 | tf_op jit(solution)/shard_map/jit(_take)/gather | solution.py:110
  46.5 25.8 %all_gather.16 = bf16[4,2048]{1,0:T(4,128)(2,1)S(1)} all-gather(bf16[4,128]{1,0:T(4,128)(2,1)S(1)} %broadcast_select_fusion.2), channel_id=1, replica_groups=mesh['group'=8,'head'=16] {'head'}, dimensions={1}, use_global_device_ids=true | all-gather | bytes 17408 | tf_op jit(solution)/shard_map/all_gather | solution.py:113
  73.7 29.2 %all_gather.18 = bf16[128,2048]{1,0:T(8,128)(2,1)S(1)} all-gather(bf16[128,256]{1,0:T(8,128)(2,1)S(1)} %convert_element_type.102), channel_id=1, replica_groups=mesh['group'=8,'head'=16] {'group'}, dimensions={1}, use_global_device_ids=true | all-gather | bytes 589824 | tf_op jit(solution)/shard_map/all_gather | solution.py:122
  108.8 5.7 all-gather.4.cloned.1.call-done
  114.4 3.0 convert_reduce_fusion
  117.4 3.4 fusion.32
  121.8 1.9 pad_maximum_fusion
  123.7 2.2 copy-done.8
  125.8 2.5 bitcast_subtract_fusion.2
  128.4 2.5 fusion.49
  131.6 8.0 %fusion.56 = bf16[1024,64]{0,1:T(8,128)(2,1)S(1)} fusion(bf16[2048,64]{0,1:T(8,128)(2,1)S(1)} %copy-done.20, f32[1024,2048]{1,0:T(8,128)} %copy-done.4, bf16[1024,2048]{1,0:T(8,128)(2,1)} %all-gather.4.cloned.1.call-done, f32[2048]{0:T(1024)S(1)} %bitcast.328, f32[1024]{0:T(1024)S(1)} %add_rsqrt_fusion.1, f32[1024]{0:T(1024)S(1)} %broadcast_multiply_fusion.2, ...), kind=kOutput, calls=%fused_computation.107 | convolution fusion | flops 417398784 | bytes 13189120 | tf_op jit(solution)/shard_map/dot_general | solution.py:55
  141.0 6.1 add_convert_fusion.3
  149.5 3.4 add_convert_fusion.4
  154.4 3.6 add_convert_fusion.5
  159.5 67.9 %while.32 = (s32[]{:T(128)}, f32[2,64,64]{2,1,0:T(8,128)S(1)}, f32[2,64]{1,0:T(2,128)S(1)}, f32[8,2,128,64]{2,3,0,1:T(8,128)}, f32[8,2,128,64]{3,2,0,1:T(8,128)}...) while((s32[]{:T(128)}, f32[2,64,64]{2,1,0:T(8,128)S(1)}, ...), condition=%wide.region_12.14_spmd.clone, body=%wide.region_9.13_spmd.clone.sunk | while | flops 77955200 | bytes 2999012 | solution.py:189
  164.0 1.7 fusion.134
  165.6 1.7 bitcast_dynamic-update-slice_fusion.4
  172.5 1.7 fusion.134
  174.1 1.7 bitcast_dynamic-update-slice_fusion.4
  180.9 1.7 fusion.134
  182.6 1.7 bitcast_dynamic-update-slice_fusion.4
  189.4 1.7 fusion.134
  191.1 1.7 bitcast_dynamic-update-slice_fusion.4
  197.9 1.7 fusion.134
  199.6 1.7 bitcast_dynamic-update-slice_fusion.4
  206.4 1.7 fusion.134
  208.0 1.7 bitcast_dynamic-update-slice_fusion.4
  214.8 1.7 fusion.134
  216.5 1.7 bitcast_dynamic-update-slice_fusion.4
  223.4 1.7 fusion.134
  225.0 1.7 bitcast_dynamic-update-slice_fusion.4
  229.0 43.0 %while.33 = (s32[]{:T(128)}, f32[2,64,64]{2,1,0:T(8,128)S(1)}, f32[2,64]{1,0:T(2,128)S(1)}, f32[2,64,64]{2,1,0:T(8,128)S(1)}, s32[]{:T(128)}, /*index=5*/s32[]{:T(128)}) while((s32[]{:T(128)}, f32[2,64,64]{2,1,0:T(8,128)S(1)}, f32[2,64]{1,0:T(2,128)S(1)}, f32[2,64,64]{2,1,0:T(8,128)S(1)}, s32[]{:T(128)}, ...), condition=%wide.region_14.16_spmd.clone, body=%wide.region_13.15_spmd.clone.sunk | while | flops 40963 | bytes 197239 | solution.py:212
  229.1 2.1 collective-permute-start
  231.2 1.6 collective-permute-done
  232.9 4.2 collective-permute-start
  237.1 1.6 collective-permute-done
  238.8 4.2 collective-permute-start
  243.0 1.6 collective-permute-done
  244.7 4.2 collective-permute-start
  248.9 1.6 collective-permute-done
  250.6 4.2 collective-permute-start
  254.8 1.6 collective-permute-done
  256.5 5.9 collective-permute-start
  262.4 1.6 collective-permute-done
  264.0 6.3 %collective-permute-start = (bf16[2,64,64]{2,1,0:T(8,128)(2,1)S(1)}, bf16[2,64,64]{2,1,0:T(8,128)(2,1)S(1)}, u32[]{:S(2)}, u32[]{:S(2)}) collective-permute-start(bf16[2,64,64]{2,1,0:T(8,128)(2,1)S(1)} %fusion.135), channel_id=1, source_target_pairs={{0,16},{16,32},{32,48},{48,64},{64,80},{80,96},{96,112},{1,17},{17... | collective-permute-start | bytes 49160 | tf_op jit(solution)/shard_map/while/body/eval_jaxpr/ppermute | solution.py:25
  270.4 1.6 collective-permute-done
  272.0 2.6 fusion.109
  278.1 7.8 %multiply_convert_fusion.1 = bf16[1024,128]{1,0:T(8,128)(2,1)S(1)} fusion(bf16[5,2048,128]{2,1,0:T(8,128)(2,1)} %all-gather.6.cloned.1.call-done, f32[1024,2048]{1,0:T(8,128)} %copy-done.4, bf16[1024,2048]{1,0:T(8,128)(2,1)} %all-gather.4.cloned.1.call-done, f32[2048]{0:T(1024)S(1)} %bitcast.327, f32[1024]{0:T(1024)S(1)} %add_rsqrt_fusion.1, ...), kind=kOutput, calls=%fused_computation.114 | convolution fusion | flops 686948352 | bytes 15155712 | tf_op jit(solution)/shard_map/dot_general | solution.py:140
  285.9 3.2 convolution_convert_fusion.1
  290.5 14.9 %all-to-all-start = ((bf16[8,448,256]{2,1,0:T(8,128)(2,1)}), bf16[8,448,256]{2,1,0:T(8,128)(2,1)S(1)}, u32[]{:S(2)}, u32[]{:S(2)}) async-start(bf16[8,448,256]{2,1,0:T(8,128)(2,1)} %stack.4), calls=%async_computation | async-start | bytes 3670016 | tf_op jit(solution)/shard_map/all_to_all | solution.py:18
  306.9 16.0 %all-to-all-done = bf16[8,448,256]{2,1,0:T(8,128)(2,1)S(1)} async-done(((bf16[8,448,256]{2,1,0:T(8,128)(2,1)}), bf16[8,448,256]{2,1,0:T(8,128)(2,1)S(1)}, u32[]{:S(2)}, u32[]{:S(2)}) %all-to-all-start) | async-done | bytes 1835040 | tf_op jit(solution)/shard_map/all_to_all | solution.py:18
  324.4 133.7 %all-reduce.2.cloned.1.call-done = bf16[1024,2048]{1,0:T(8,128)(2,1)} async-done(((bf16[1024,2048]{1,0:T(8,128)(2,1)}), bf16[1024,2048]{1,0:T(8,128)(2,1)}) %all-reduce.2.cloned.1.call-update) | async-done | bytes 4194320 | tf_op jit(solution)/shard_map/psum | solution.py:219
  458.1 4.8 convert_reduce_fusion.1
  464.1 3.6 collective-permute-start.1
  468.7 3.2 copy-done.7
  474.6 4.7 pad_maximum_fusion.1
  479.3 4.5 bitcast_subtract_fusion.1
  483.8 19.4 %all-gather.8.cloned.1.call-done = bf16[2048,448]{0,1:T(8,128)(2,1)} async-done(((bf16[256,448]{0,1:T(8,128)(2,1)}), bf16[2048,448]{0,1:T(8,128)(2,1)}) %all-gather.8.cloned.1.call-update) | async-done | bytes 1835024 | tf_op jit(solution)/shard_map/all_gather | solution.py:121
  503.2 11.7 %convolution_convert_fusion = bf16[1024,2048]{1,0:T(8,128)(2,1)} fusion(bf16[448,2048]{1,0:T(8,128)(2,1)S(1)} %bitcast.310, bf16[2048,448]{0,1:T(8,128)(2,1)} %all-gather.8.cloned.1.call-done, f32[1024,2048]{1,0:T(8,128)} %bitcast_subtract_fusion.1, f32[2048]{0:T(1024)S(1)} %bitcast.326, bf16[1024,2048]{1,0:T(8,128)(2,1)} %copy-done.5, ...), kind=kOutput, calls=%fused_computation.83 | convolution fusion | flops 3774152704 | bytes 20463616 | tf_op jit(solution)/shard_map/dot_general | solution.py:242
  515.0 6.5 %copy.118 = bf16[1024,2048]{0,1:T(8,128)(2,1)} copy(bf16[1024,2048]{1,0:T(8,128)(2,1)} %convolution_convert_fusion) | data formatting | bytes 8388608
  526.0 78.4 %reduce-scatter.4.cloned.1.call-done = bf16[128,1024]{1,0:T(8,128)(2,1)} async-done(((bf16[2048,1024]{1,0:T(8,128)(2,1)}), bf16[128,1024]{1,0:T(8,128)(2,1)}) %reduce-scatter.4.cloned.1.call-update) | async-done | bytes 262160
  605.6 7.3 %fusion.57 = bf16[1024,128]{1,0:T(8,128)(2,1)} fusion(f32[1024,2048]{1,0:T(8,128)} %bitcast_subtract_fusion.1, f32[2048]{0:T(1024)S(1)} %bitcast.325, bf16[5,2048,128]{2,1,0:T(8,128)(2,1)} %all-gather.6.cloned.1.call-done, bf16[1024,128]{1,0:T(8,128)(2,1)S(1)} %copy.119, bf16[1024,2048]{1,0:T(8,128)(2,1)} %copy-done.5, s32[]{:T(128)S(6)} %select_n.209, ...), kind=kOutput, calls=%fused_computation.108 | convolution fusion | flops 550633472 | bytes 13911044 | tf_op jit(solution)/shard_map/dot_general | solution.py:238
  (311 shorter events, 91.9 us)
Async XLA Ops:
  7.2 121.2 %copy-start = (bf16[2048,160]{0,1:T(8,128)(2,1)S(1)}, bf16[2048,160]{0,1:T(8,128)(2,1)}, u32[]{:S(2)}) copy-start(bf16[2048,160]{0,1:T(8,128)(2,1)} %param.28) | copy-start | bytes 1966084
  7.2 97.0 %all-gather.6.cloned.1.call-start = ((), (), s32[]{:S(2)}) async-start(), calls=%async_computation.3 | async-start | bytes 2949120 | tf_op jit(solution)/shard_map/all_gather | solution.py:120
  9.2 105.3 %all-gather.4.cloned.1.call-start = ((), (), s32[]{:S(2)}) async-start(), calls=%async_computation.2 | async-start | bytes 4456448 | tf_op jit(solution)/shard_map/all_gather | solution.py:112
  27.2 430.9 %all-reduce.2.cloned.1.call-start = ((), (), s32[]{:S(2)}) async-start(), calls=%async_computation.4 | async-start | bytes 8388608 | tf_op jit(solution)/shard_map/psum | solution.py:219
  114.4 6.4 %copy-start.2 = (bf16[1024,2048]{1,0:T(8,128)(2,1)S(1)}, bf16[1024,2048]{1,0:T(8,128)(2,1)}, u32[]{:S(2)}) copy-start(bf16[1024,2048]{1,0:T(8,128)(2,1)} %all-gather.4.cloned.1.call-done) | copy-start | bytes 12582916
  121.8 4.1 copy-start.8
  128.4 3.2 copy-start.4
  128.4 3.2 copy-start.16
  128.4 3.2 copy-start.20
  131.6 9.4 %copy-start.17 = (bf16[1024,160]{0,1:T(8,128)(2,1)}, bf16[1024,160]{0,1:T(8,128)(2,1)S(1)}, u32[]{:S(2)}) copy-start(bf16[1024,160]{0,1:T(8,128)(2,1)S(1)} %fusion.49) | copy-start | bytes 983044
  131.6 8.0 %copy-start.18 = (bf16[64,128]{1,0:T(8,128)(2,1)S(1)}, bf16[64,128]{1,0:T(8,128)(2,1)}, u32[]{:S(2)}) copy-start(bf16[64,128]{1,0:T(8,128)(2,1)} %param.31) | copy-start | bytes 49156
  131.6 8.0 %copy-start.19 = (f32[128]{0:T(128)S(1)}, f32[128]{0:T(128)}, u32[]{:S(2)}) copy-start(f32[128]{0:T(128)} %param.32) | copy-start | bytes 1540
  141.0 7.7 %slice-start = ((s8[8388608]{0:T(1024)(128)(4,1)}), s8[4194304]{0:T(1024)(128)(4,1)S(1)}, s32[]{:S(2)}) async-start(s8[8388608]{0:T(1024)(128)(4,1)} %bitcast.290), calls=%async_computation.7 | async-start | bytes 8388608
  141.0 6.2 copy-start.11
  141.0 7.7 %copy-start.3 = (bf16[1024,2048]{1,0:T(8,128)(2,1)S(1)}, bf16[1024,2048]{1,0:T(8,128)(2,1)}, u32[]{:S(2)}) copy-start(bf16[1024,2048]{1,0:T(8,128)(2,1)} %all-gather.4.cloned.1.call-done) | copy-start | bytes 12582916
  141.0 8.4 %slice-start.1 = ((s8[8388608]{0:T(1024)(128)(4,1)}), s8[4194304]{0:T(1024)(128)(4,1)S(1)}, s32[]{:S(2)}) async-start(s8[8388608]{0:T(1024)(128)(4,1)} %bitcast.290), calls=%async_computation.8 | async-start | bytes 8388608
  149.4 3.4 copy-start.10
  154.4 3.6 copy-start.9
  154.4 5.1 copy-start.21
  227.4 50.7 %copy-start.22 = (f32[128]{0:T(128)S(1)}, f32[128]{0:T(128)}, u32[]{:S(2)}) copy-start(f32[128]{0:T(128)} %param.34) | copy-start | bytes 1540
  229.1 3.7 collective-permute-start
  232.9 5.8 collective-permute-start
  238.8 5.8 collective-permute-start
  244.7 5.8 collective-permute-start
  250.6 5.8 collective-permute-start
  256.5 7.4 %collective-permute-start = (bf16[2,64,64]{2,1,0:T(8,128)(2,1)S(1)}, bf16[2,64,64]{2,1,0:T(8,128)(2,1)S(1)}, u32[]{:S(2)}, u32[]{:S(2)}) collective-permute-start(bf16[2,64,64]{2,1,0:T(8,128)(2,1)S(1)} %fusion.135), channel_id=1, source_target_pairs={{0,16},{16,32},{32,48},{48,64},{64,80},{80,96},{96,112},{1,17},{17... | collective-permute-start | bytes 49160 | tf_op jit(solution)/shard_map/while/body/eval_jaxpr/ppermute | solution.py:25
  264.0 7.9 %collective-permute-start = (bf16[2,64,64]{2,1,0:T(8,128)(2,1)S(1)}, bf16[2,64,64]{2,1,0:T(8,128)(2,1)S(1)}, u32[]{:S(2)}, u32[]{:S(2)}) collective-permute-start(bf16[2,64,64]{2,1,0:T(8,128)(2,1)S(1)} %fusion.135), channel_id=1, source_target_pairs={{0,16},{16,32},{32,48},{48,64},{64,80},{80,96},{96,112},{1,17},{17... | collective-permute-start | bytes 49160 | tf_op jit(solution)/shard_map/while/body/eval_jaxpr/ppermute | solution.py:25
  285.9 3.2 copy-start.14
  289.1 16.4 %copy-start.15 = (f32[256,448]{0,1:T(8,128)S(1)}, f32[256,448]{0,1:T(8,128)}, u32[]{:S(2)}) copy-start(f32[256,448]{0,1:T(8,128)} %param.24) | copy-start | bytes 1376260
  290.5 32.3 %all-to-all-start = ((bf16[8,448,256]{2,1,0:T(8,128)(2,1)}), bf16[8,448,256]{2,1,0:T(8,128)(2,1)S(1)}, u32[]{:S(2)}, u32[]{:S(2)}) async-start(bf16[8,448,256]{2,1,0:T(8,128)(2,1)} %stack.4), calls=%async_computation | async-start | bytes 3670016 | tf_op jit(solution)/shard_map/all_to_all | solution.py:18
  305.4 197.8 %all-gather.8.cloned.1.call-start = ((), (), s32[]{:S(2)}) async-start(), calls=%async_computation.5 | async-start | bytes 2064384 | tf_op jit(solution)/shard_map/all_gather | solution.py:121
  306.2 298.2 %reduce-scatter.4.cloned.1.call-start = ((), (), s32[]{:S(2)}) async-start(), calls=%async_computation.6 | async-start | bytes 4456448
  462.8 5.8 copy-start.5
  464.1 7.8 %collective-permute-start.1 = (bf16[1,2048]{1,0:T(2,128)(2,1)S(1)}, bf16[1,2048]{1,0:T(2,128)(2,1)S(1)}, u32[]{:S(2)}, u32[]{:S(2)}) collective-permute-start(bf16[1,2048]{1,0:T(2,128)(2,1)S(1)} %constant_dynamic-slice_fusion.5), channel_id=1, source_target_pairs={{0,16},{16,32},{32,48},{48,64},{64,80},{80,96},{96,112},{1,17},{17... | collective-permute-start | bytes 12296 | tf_op jit(solution)/shard_map/ppermute | solution.py:25
  468.6 3.2 copy-start.7
  474.6 4.7 copy-start.6
  479.3 24.0 %copy-start.12 = (bf16[8,56,8,256]{3,2,0,1:T(8,128)(2,1)S(1)}, bf16[8,56,8,256]{3,2,0,1:T(8,128)(2,1)}, u32[]{:S(2)}) copy-start(bf16[8,56,8,256]{3,2,0,1:T(8,128)(2,1)} %copy.138) | copy-start | bytes 5505028
  515.0 8.2 %copy-start.13 = (f32[8,2,64,64]{3,2,1,0:T(8,128)S(1)}, f32[8,2,64,64]{3,2,1,0:T(8,128)}, u32[]{:S(2)}) copy-start(f32[8,2,64,64]{3,2,1,0:T(8,128)} %get-tuple-element.108) | copy-start | bytes 786436
  604.4 8.5 %copy-start.1 = (bf16[2048,160]{0,1:T(8,128)(2,1)S(1)}, bf16[2048,160]{0,1:T(8,128)(2,1)}, u32[]{:S(2)}) copy-start(bf16[2048,160]{0,1:T(8,128)(2,1)} %param.28) | copy-start | bytes 1966084
Sparse Core Ops, SparseCore 0:
  9.6 44.0 all-gather.5
  56.5 57.8 all-gather.3
  289.2 168.8 all-reduce.1
  460.1 43.1 all-gather.7
  521.6 82.7 reduce-scatter.3
